TPU v7x, 512 devices: a whole 4x8x8 slice. The times are simulated.
512 devices in a mesh: ctx: 64 (over y, z_lo, core), dp: 8 (over z_hi, x).
Axes of the slice: x: 4, y: 8, z: 8 (z_hi: 2, z_lo: 4; z = z_hi * 4 + z_lo), core: 2. Of those that a mesh axis runs over, the one named last changes fastest.
Arguments:
- features: bfloat16 [8, 12288, 1536], P('dp', 'ctx'), may hold values from -6 to 6
- bottleneck: bfloat16 [8, 12288, 384], P('dp', 'ctx'), may hold values from -6 to 6
- node_noise: bfloat16 [8, 12288, 1536], P('dp', 'ctx'), may hold values from -6 to 6
- targets: bfloat16 [8, 12288, 1536], P('dp', 'ctx'), may hold values from -15 to 15
- entry_weight: bfloat16 [384, 1536], P('ctx'), may hold values from -0.3125 to 0.3125
- conv_filters: bfloat16 [3, 1536, 384], P(None, None, 'ctx'), may hold values from -0.09375 to 0.09375
- exit_weight: bfloat16 [384, 1536], P('ctx'), may hold values from -0.3125 to 0.3125
Outputs:
- blended: bfloat16 [8, 12288, 1536], P('dp', 'ctx')
- estimate: float32 [384, 1536], P('ctx')
All inputs are finite; a program needn't handle non-finite values.
Results may differ from a plain program's by a relative error of at most 0.015.
The roundings to bfloat16 on the way count: a program that leaves them out, or rounds other values in their place, can miss the bound.
Values may be sent and summed in bfloat16 or wider, within the bound.
No kernel may reach another device: no remote copies, remote signals or barrier semaphores. Data moves between devices by JAX's collectives and lax.ppermute only.
A program may use at most 64 MiB of HBM per device.

v0:
```python
import jax
import jax.numpy as jnp
from jax import lax
from jax.sharding import PartitionSpec as P

DILATION = 32
NOISE_SCALE = 0.1


def padded_2(cells, sides, width):
    for axis, dim in sides:
        count = lax.axis_size(axis)
        ends = count - 1
        head = lax.slice_in_dim(cells, 0, width, axis=dim)
        tail = lax.slice_in_dim(cells, cells.shape[dim] - width, cells.shape[dim], axis=dim)
        cells = jnp.concatenate(
            [
                lax.ppermute(tail, axis, [(i, (i + 1) % count) for i in range(ends)]),
                cells,
                lax.ppermute(head, axis, [((i + 1) % count, i) for i in range(ends)]),
            ],
            axis=dim,
        )
    return cells


def taps_for(padded, row_count, spacing, portion):
    summed = jnp.dot(padded[..., 0:row_count, :], portion[0], preferred_element_type=jnp.float32)
    summed = summed + jnp.dot(
        padded[..., spacing : spacing + row_count, :],
        portion[1],
        preferred_element_type=jnp.float32,
    )
    summed = summed + jnp.dot(
        padded[..., 2 * spacing : 2 * spacing + row_count, :],
        portion[2],
        preferred_element_type=jnp.float32,
    )
    return summed


def rows_for(left_side, portion):
    return jnp.dot(left_side, portion, preferred_element_type=jnp.float32)


def body(features, bottleneck, node_noise, targets, entry_weight, conv_filters, exit_weight):
    feats = features[0]
    bottle = bottleneck[0]
    jitter = node_noise[0]
    goal = targets[0].astype(jnp.float32)
    row_count = feats.shape[0]
    chan_count = feats.shape[1]
    spacing = DILATION
    baseline = feats.astype(jnp.float32) + rows_for(
        bottle, lax.all_gather(entry_weight, "ctx", axis=0, tiled=True)
    )
    offset_field = jitter.astype(jnp.float32) * NOISE_SCALE
    results = []
    for polarity in (1.0, -1.0):
        state = baseline + polarity * offset_field
        activated = jax.nn.gelu(state).astype(jnp.bfloat16)
        padded = padded_2(activated, (("ctx", 0),), spacing)
        mixed = taps_for(
            padded, row_count, spacing, lax.all_gather(conv_filters, "ctx", axis=2, tiled=True)
        )
        inner = jax.nn.gelu(mixed).astype(jnp.bfloat16)
        results.append(
            state + rows_for(inner, lax.all_gather(exit_weight, "ctx", axis=0, tiled=True))
        )
    upper = results[0]
    lower = results[1]
    blended = ((upper + lower) * 0.5).astype(jnp.bfloat16)[None]
    local_gap = jnp.sum((upper - lower) * (upper + lower - 2.0 * goal)) / (
        row_count * lax.axis_size("ctx") * chan_count
    )
    factor = lax.psum(local_gap, "ctx") / (2.0 * NOISE_SCALE)
    local_term = factor * lax.dot_general(
        bottle, jitter, (((0,), (0,)), ((), ())), preferred_element_type=jnp.float32
    )
    grouped = lax.psum(local_term, "dp")
    estimate = lax.psum_scatter(grouped, "ctx", scatter_dimension=0, tiled=True)
    return (blended, estimate)


def solution(mesh):
    return jax.shard_map(
        body,
        mesh=mesh,
        in_specs=(
            P("dp", "ctx", None),
            P("dp", "ctx", None),
            P("dp", "ctx", None),
            P("dp", "ctx", None),
            P("ctx", None),
            P(None, None, "ctx"),
            P("ctx", None),
        ),
        out_specs=(P("dp", "ctx", None), P("ctx", None)),
        check_vma=False,
    )
```

profile of v0, /device:TPU:8, one launch (start us, length us, event | category | flops | bytes accessed | tf_op | source)
XLA Modules:
  0.0 814.6 jit_solution(17729310585328299950)
XLA Ops:
  7.2 0.0 copy-start
  7.2 0.0 all-gather.8.cloned.1.call-start
  7.2 0.7 all-gather.8.cloned.1.call-update
  7.9 0.0 all-gather.10.cloned.1.call-start
  8.0 0.7 all-gather.10.cloned.1.call-update
  8.7 0.0 all-gather.6.cloned.1.call-start
  8.7 1.6 copy.10
  10.3 0.0 all-gather.6.cloned.1.call-update
  10.3 0.0 copy-start.2
  10.3 121.3 %all-gather.8.cloned.1.call-done = bf16[64,6,1536]{2,1,0:T(8,128)(2,1)} async-done(((bf16[1,6,1536]{2,1,0:T(8,128)(2,1)}), bf16[64,6,1536]{2,1,0:T(8,128)(2,1)}) %all-gather.8.cloned.1.call-update) | async-done | bytes 1179664 | tf_op jit(solution)/shard_map/all_gather | solution.py:55
  131.6 2.3 reshape.11
  133.9 3.4 fusion.18
  137.3 0.7 fusion.104
  138.0 4.7 collective-permute-start.3
  142.8 1.9 collective-permute-start.2
  144.7 0.7 fusion.105
  145.4 6.3 collective-permute-start.1
  151.7 1.9 collective-permute-start
  153.6 95.8 %all-gather.10.cloned.1.call-done = bf16[64,6,1536]{2,1,0:T(8,128)(2,1)} async-done(((bf16[1,6,1536]{2,1,0:T(8,128)(2,1)}), bf16[64,6,1536]{2,1,0:T(8,128)(2,1)}) %all-gather.10.cloned.1.call-update) | async-done | bytes 1179664 | tf_op jit(solution)/shard_map/all_gather | solution.py:68
  249.4 3.1 reshape.13
  252.5 118.6 %all-gather.6.cloned.1.call-done = bf16[3,1536,384]{1,0,2:T(4,128)(2,1)} async-done(((bf16[3,1536,6]{1,0,2:T(4,128)(2,1)}), bf16[3,1536,384]{1,0,2:T(4,128)(2,1)}) %all-gather.6.cloned.1.call-update) | async-done | bytes 3538960 | tf_op jit(solution)/shard_map/all_gather | solution.py:64
  371.1 12.6 %fusion.103 = (bf16[1,1536,384]{1,0,2:T(2,128)(2,1)}, bf16[1,1536,384]{1,0,2:T(2,128)(2,1)}, bf16[1,1536,384]{1,0,2:T(2,128)(2,1)}) fusion(bf16[3,1536,384]{1,0,2:T(4,128)(2,1)} %all-gather.6.cloned.1.call-done), kind=kLoop, calls=%fused_computation.97 | loop fusion | bytes 7077888 | tf_op jit(solution)/shard_map/slice | solution.py:28
  383.7 5.6 copy.15
  389.3 0.5 fusion.25
  389.8 6.5 copy.16
  396.3 0.0 collective-permute-done.3
  396.4 2.5 fusion.21
  398.9 5.6 copy.14
  404.5 0.0 collective-permute-done.2
  404.5 3.9 convolution_add_fusion
  408.4 1.7 fusion.27
  410.1 2.2 fusion.23
  412.2 0.0 collective-permute-done
  412.2 4.6 fusion.20
  417.4 119.0 %psum.14 = f32[]{:T(128)} all-reduce(f32[]{:T(128)S(6)} %div.6), channel_id=1, replica_groups=mesh['ctx'=64,'dp'=8] {'ctx'}, use_global_device_ids=true, to_apply=%region_1.0 | all-reduce | flops 1 | bytes 8 | tf_op jit(solution)/shard_map/psum | solution.py:76
  537.1 0.5 convolution_multiply_fusion
  537.6 149.7 %fusion = f32[8,1536]{1,0:T(8,128)S(1)} fusion(f32[384,1536]{1,0:T(8,128)S(1)} %convolution_multiply_fusion), kind=kCustom, calls=%all-reduce-scatter | all-reduce-scatter fusion | flops 786433 | bytes 2410496
  687.3 2.0 collective-permute-start.19
  689.2 21.3 %collective-permute-start.10 = (f32[8,1536]{1,0:T(8,128)S(1)}, f32[8,1536]{1,0:T(8,128)S(1)}, u32[]{:S(2)}, u32[]{:S(2)}) collective-permute-start(f32[8,1536]{1,0:T(8,128)S(1)} %fusion), channel_id=1, source_target_pairs={{0,56},{8,64},{16,72},{24,80},{32,88},{40,96},{48,104},{56,112},{6... | collective-permute-start | bytes 147464
  710.5 5.5 collective-permute-start.11
  716.0 1.9 collective-permute-start.12
  717.9 2.3 collective-permute-start.13
  720.3 1.3 collective-permute-start.14
  721.6 0.0 collective-permute-done.10
  721.6 5.7 collective-permute-start.15
  727.3 1.6 collective-permute-start.16
  728.9 0.0 collective-permute-done.12
  728.9 2.7 collective-permute-start.17
  731.7 1.4 collective-permute-start.18
  733.1 2.0 collective-permute-start.4
  735.0 0.0 collective-permute-done.15
  735.1 3.0 collective-permute-start.5
  738.1 2.7 collective-permute-start.6
  740.8 0.0 collective-permute-done.17
  740.8 4.1 collective-permute-start.7
  744.9 0.0 collective-permute-done.18
  744.9 1.9 collective-permute-start.8
  746.9 3.9 collective-permute-start.9
  750.8 1.3 dynamic-slice.4
  752.7 0.0 collective-permute-done.5
  752.7 0.0 collective-permute-done.8
  752.7 1.0 collective-permute-done.9
  753.7 1.9 concatenate.18
  755.6 52.5 %psum.16 = f32[6,1536]{1,0:T(8,128)} all-reduce(f32[6,1536]{1,0:T(8,128)S(1)} %constant_dynamic-slice_fusion), channel_id=1, replica_groups=mesh['ctx'=64,'dp'=8] {'dp'}, use_global_device_ids=true, to_apply=%region_2.0 | all-reduce | flops 9216 | bytes 73728 | tf_op jit(solution)/shard_map/psum | solution.py:80
  (23 shorter events, 0.1 us)
Async XLA Ops:
  7.2 126.7 %copy-start = (bf16[1,192,384]{2,1,0:T(8,128)(2,1)S(1)}, bf16[1,192,384]{2,1,0:T(8,128)(2,1)}, u32[]{:S(2)}) copy-start(bf16[1,192,384]{2,1,0:T(8,128)(2,1)} %param.8) | copy-start | bytes 442372
  7.2 124.4 %all-gather.8.cloned.1.call-start = ((), (), s32[]{:S(2)}) async-start(), calls=%async_computation.1 | async-start | bytes 1597440 | tf_op jit(solution)/shard_map/all_gather | solution.py:55
  7.9 241.5 %all-gather.10.cloned.1.call-start = ((), (), s32[]{:S(2)}) async-start(), calls=%async_computation.2 | async-start | bytes 1597440 | tf_op jit(solution)/shard_map/all_gather | solution.py:68
  8.7 362.4 %all-gather.6.cloned.1.call-start = ((), (), s32[]{:S(2)}) async-start(), calls=%async_computation | async-start | bytes 4792320 | tf_op jit(solution)/shard_map/all_gather | solution.py:64
  10.3 123.6 %copy-start.2 = (bf16[1,192,1536]{2,1,0:T(8,128)(2,1)S(1)}, bf16[1,192,1536]{2,1,0:T(8,128)(2,1)}, u32[]{:S(2)}) copy-start(bf16[1,192,1536]{2,1,0:T(8,128)(2,1)} %param.9) | copy-start | bytes 1769476
  137.3 115.2 %copy-start.4 = (bf16[192,1536]{1,0:T(8,128)(2,1)}, bf16[192,1536]{1,0:T(8,128)(2,1)S(1)}, u32[]{:S(2)}) copy-start(bf16[192,1536]{1,0:T(8,128)(2,1)S(1)} %get-tuple-element.8) | copy-start | bytes 1769476
  137.3 259.1 %copy-start.3 = (bf16[192,1536]{1,0:T(8,128)(2,1)}, bf16[192,1536]{1,0:T(8,128)(2,1)S(1)}, u32[]{:S(2)}) copy-start(bf16[192,1536]{1,0:T(8,128)(2,1)S(1)} %get-tuple-element.7) | copy-start | bytes 1769476
  138.0 258.3 %collective-permute-start.3 = (bf16[32,1536]{1,0:T(8,128)(2,1)}, bf16[32,1536]{1,0:T(8,128)(2,1)}, u32[]{:S(2)}, u32[]{:S(2)}) collective-permute-start(bf16[32,1536]{1,0:T(8,128)(2,1)} %get-tuple-element.10), channel_id=1, source_target_pairs={{8,0},{16,8},{24,16},{32,24},{40,32},{48,40},{56,48},{64,56},{72,6... | collective-permute-start | bytes 294920 | tf_op jit(solution)/shard_map/ppermute | solution.py:20
  142.8 261.7 %collective-permute-start.2 = (bf16[32,1536]{1,0:T(8,128)(2,1)}, bf16[32,1536]{1,0:T(8,128)(2,1)}, u32[]{:S(2)}, u32[]{:S(2)}) collective-permute-start(bf16[32,1536]{1,0:T(8,128)(2,1)} %get-tuple-element.9), channel_id=1, source_target_pairs={{0,8},{8,16},{16,24},{24,32},{32,40},{40,48},{48,56},{56,64},{64,7... | collective-permute-start | bytes 294920 | tf_op jit(solution)/shard_map/ppermute | solution.py:18
  145.4 264.7 %collective-permute-start.1 = (bf16[32,1536]{1,0:T(8,128)(2,1)}, bf16[32,1536]{1,0:T(8,128)(2,1)}, u32[]{:S(2)}, u32[]{:S(2)}) collective-permute-start(bf16[32,1536]{1,0:T(8,128)(2,1)} %get-tuple-element.12), channel_id=1, source_target_pairs={{8,0},{16,8},{24,16},{32,24},{40,32},{48,40},{56,48},{64,56},{72,6... | collective-permute-start | bytes 294920 | tf_op jit(solution)/shard_map/ppermute | solution.py:20
  151.7 260.5 %collective-permute-start = (bf16[32,1536]{1,0:T(8,128)(2,1)}, bf16[32,1536]{1,0:T(8,128)(2,1)S(1)}, u32[]{:S(2)}, u32[]{:S(2)}) collective-permute-start(bf16[32,1536]{1,0:T(8,128)(2,1)} %get-tuple-element.11), channel_id=1, source_target_pairs={{0,8},{8,16},{16,24},{24,32},{32,40},{40,48},{48,56},{56,64},{64,7... | collective-permute-start | bytes 294920 | tf_op jit(solution)/shard_map/ppermute | solution.py:18
  408.4 1.7 copy-start.5
  408.4 1.7 copy-start.6
  410.0 2.2 copy-start.1
  687.3 33.0 %collective-permute-start.19 = (f32[6,1536]{1,0:T(8,128)S(1)}, f32[6,1536]{1,0:T(8,128)S(1)}, u32[]{:S(2)}, u32[]{:S(2)}) collective-permute-start(f32[6,1536]{1,0:T(8,128)S(1)} %slice.58), channel_id=1, source_target_pairs={{0,128},{8,136},{16,144},{24,152},{32,160},{40,168},{48,176},{56,1... | collective-permute-start | bytes 110600
  689.2 32.3 %collective-permute-start.10 = (f32[8,1536]{1,0:T(8,128)S(1)}, f32[8,1536]{1,0:T(8,128)S(1)}, u32[]{:S(2)}, u32[]{:S(2)}) collective-permute-start(f32[8,1536]{1,0:T(8,128)S(1)} %fusion), channel_id=1, source_target_pairs={{0,56},{8,64},{16,72},{24,80},{32,88},{40,96},{48,104},{56,112},{6... | collective-permute-start | bytes 147464
  710.5 16.8 %collective-permute-start.11 = (f32[8,1536]{1,0:T(8,128)S(1)}, f32[8,1536]{1,0:T(8,128)S(1)}, u32[]{:S(2)}, u32[]{:S(2)}) collective-permute-start(f32[8,1536]{1,0:T(8,128)S(1)} %fusion), channel_id=1, source_target_pairs={{0,64},{8,72},{16,80},{24,88},{32,96},{40,104},{48,112},{56,120},{... | collective-permute-start | bytes 147464
  716.0 12.9 %collective-permute-start.12 = (f32[8,1536]{1,0:T(8,128)S(1)}, f32[8,1536]{1,0:T(8,128)S(1)}, u32[]{:S(2)}, u32[]{:S(2)}) collective-permute-start(f32[8,1536]{1,0:T(8,128)S(1)} %fusion), channel_id=1, source_target_pairs={{0,72},{8,80},{16,88},{24,96},{32,104},{40,112},{48,120},{56,128},... | collective-permute-start | bytes 147464
  717.9 13.8 %collective-permute-start.13 = (f32[8,1536]{1,0:T(8,128)S(1)}, f32[8,1536]{1,0:T(8,128)S(1)}, u32[]{:S(2)}, u32[]{:S(2)}) collective-permute-start(f32[8,1536]{1,0:T(8,128)S(1)} %fusion), channel_id=1, source_target_pairs={{0,80},{8,88},{16,96},{24,104},{32,112},{40,120},{48,128},{56,136}... | collective-permute-start | bytes 147464
  720.3 12.8 %collective-permute-start.14 = (f32[8,1536]{1,0:T(8,128)S(1)}, f32[8,1536]{1,0:T(8,128)S(1)}, u32[]{:S(2)}, u32[]{:S(2)}) collective-permute-start(f32[8,1536]{1,0:T(8,128)S(1)} %fusion), channel_id=1, source_target_pairs={{0,88},{8,96},{16,104},{24,112},{32,120},{40,128},{48,136},{56,144... | collective-permute-start | bytes 147464
  721.6 13.5 %collective-permute-start.15 = (f32[8,1536]{1,0:T(8,128)S(1)}, f32[8,1536]{1,0:T(8,128)S(1)}, u32[]{:S(2)}, u32[]{:S(2)}) collective-permute-start(f32[8,1536]{1,0:T(8,128)S(1)} %fusion), channel_id=1, source_target_pairs={{0,96},{8,104},{16,112},{24,120},{32,128},{40,136},{48,144},{56,15... | collective-permute-start | bytes 147464
  727.3 10.8 %collective-permute-start.16 = (f32[8,1536]{1,0:T(8,128)S(1)}, f32[8,1536]{1,0:T(8,128)S(1)}, u32[]{:S(2)}, u32[]{:S(2)}) collective-permute-start(f32[8,1536]{1,0:T(8,128)S(1)} %fusion), channel_id=1, source_target_pairs={{0,104},{8,112},{16,120},{24,128},{32,136},{40,144},{48,152},{56,1... | collective-permute-start | bytes 147464
  728.9 11.9 %collective-permute-start.17 = (f32[8,1536]{1,0:T(8,128)S(1)}, f32[8,1536]{1,0:T(8,128)S(1)}, u32[]{:S(2)}, u32[]{:S(2)}) collective-permute-start(f32[8,1536]{1,0:T(8,128)S(1)} %fusion), channel_id=1, source_target_pairs={{0,112},{8,120},{16,128},{24,136},{32,144},{40,152},{48,160},{56,1... | collective-permute-start | bytes 147464
  731.7 13.2 %collective-permute-start.18 = (f32[8,1536]{1,0:T(8,128)S(1)}, f32[8,1536]{1,0:T(8,128)S(1)}, u32[]{:S(2)}, u32[]{:S(2)}) collective-permute-start(f32[8,1536]{1,0:T(8,128)S(1)} %fusion), channel_id=1, source_target_pairs={{0,120},{8,128},{16,136},{24,144},{32,152},{40,160},{48,168},{56,1... | collective-permute-start | bytes 147464
  733.1 13.8 %collective-permute-start.4 = (f32[8,1536]{1,0:T(8,128)S(1)}, f32[8,1536]{1,0:T(8,128)S(1)}, u32[]{:S(2)}, u32[]{:S(2)}) collective-permute-start(f32[8,1536]{1,0:T(8,128)S(1)} %fusion), channel_id=1, source_target_pairs={{0,8},{8,16},{16,24},{24,32},{32,40},{40,48},{48,56},{56,64},{64,7... | collective-permute-start | bytes 147464
  735.1 17.6 %collective-permute-start.5 = (f32[8,1536]{1,0:T(8,128)S(1)}, f32[8,1536]{1,0:T(8,128)S(1)}, u32[]{:S(2)}, u32[]{:S(2)}) collective-permute-start(f32[8,1536]{1,0:T(8,128)S(1)} %fusion), channel_id=1, source_target_pairs={{0,16},{8,24},{16,32},{24,40},{32,48},{40,56},{48,64},{56,72},{64,... | collective-permute-start | bytes 147464
  738.1 14.7 %collective-permute-start.6 = (f32[8,1536]{1,0:T(8,128)S(1)}, f32[8,1536]{1,0:T(8,128)S(1)}, u32[]{:S(2)}, u32[]{:S(2)}) collective-permute-start(f32[8,1536]{1,0:T(8,128)S(1)} %fusion), channel_id=1, source_target_pairs={{0,24},{8,32},{16,40},{24,48},{32,56},{40,64},{48,72},{56,80},{64,... | collective-permute-start | bytes 147464
  740.8 11.9 %collective-permute-start.7 = (f32[8,1536]{1,0:T(8,128)S(1)}, f32[8,1536]{1,0:T(8,128)S(1)}, u32[]{:S(2)}, u32[]{:S(2)}) collective-permute-start(f32[8,1536]{1,0:T(8,128)S(1)} %fusion), channel_id=1, source_target_pairs={{0,32},{8,40},{16,48},{24,56},{32,64},{40,72},{48,80},{56,88},{64,... | collective-permute-start | bytes 147464
  744.9 7.8 collective-permute-start.8
  746.9 6.9 collective-permute-start.9
Sparse Core Ops, SparseCore 0:
  10.2 121.3 all-gather.7
  133.7 115.6 all-gather.9
  251.6 119.4 all-gather.5
where the time goes:
time: 816 us; the launch traced here: 815 us
  waiting for transfers between devices  338 us (41%)
  blocking collectives  321 us (39%)
  starting transfers between devices  78.3 us (10%)
  local copies, waits for them, and re-layouts  41.9 us (5%)
  matrix products  19.1 us (2%)
  between operations  16.1 us (2%)
    unnamed x1, blocking collectives  150 us
    all_gather x1, waiting for transfers between devices, body(): lax.all_gather(entry_weight, 'ctx', axis=0, tiled=True)  121 us
    psum x1, blocking collectives, body(): factor = lax.psum(local_gap, 'ctx') / (2.0 * NOISE_SCALE)  119 us
    all_gather x1, waiting for transfers between devices, body(): lax.all_gather(conv_filters, 'ctx', axis=2, tiled=True)  119 us
    all_gather x1, waiting for transfers between devices, body(): lax.all_gather(exit_weight, 'ctx', axis=0, tiled=True)  95.8 us
    unnamed x16, starting transfers between devices  63.3 us
    psum x1, blocking collectives, body(): grouped = lax.psum(local_term, 'dp')  52.5 us
    unnamed x24, local copies, waits for them, and re-layouts  27.9 us
  transfers between devices with their start and end apart: 23, of which 4 were waited for; matrix products, arithmetic and copies ran while one was open for 7% of the time, Pallas kernels for 0%

commit v1 on v0

--- a/solution.py
+++ b/solution.py
@@ -52,7 +52,10 @@
     chan_count = feats.shape[1]
     spacing = DILATION
     baseline = feats.astype(jnp.float32) + rows_for(
-        bottle, lax.all_gather(entry_weight, "ctx", axis=0, tiled=True)
+        bottle,
+        jnp.concatenate(
+            lax.all_to_all(jnp.stack([entry_weight] * lax.axis_size("ctx")), "ctx", 0, 0), axis=0
+        ),
     )
     offset_field = jitter.astype(jnp.float32) * NOISE_SCALE
     results = []

time: 816 us -> 722 us (0.88)
  waiting for transfers between devices: 338 us -> 189 us
  blocking collectives: 321 us -> 376 us
    all_gather x1 -> x0, waiting for transfers between devices: 121 us -> none  [body(): lax.all_gather(entry_weight, 'ctx', axis=0, tiled=True)]
    all_to_all x0 -> x1, blocking collectives: none -> 54.7 us  [body(): lax.all_to_all(jnp.stack([entry_weight] * lax.axis_size('ctx')), 'ctx', 0...]
    all_gather x1, waiting for transfers between devices: 95.8 us -> 65.7 us  [body(): lax.all_gather(exit_weight, 'ctx', axis=0, tiled=True)]
    unnamed x24 -> x23, local copies, waits for them, and re-layouts: 27.9 us -> 25.6 us
  transfers between devices with their start and end apart: 23 -> 22, of which waited for: 4 -> 3; matrix products, arithmetic and copies ran while one was open for 7% -> 8% of each run, Pallas kernels for 0% -> 0%
where the time goes in v1:
time: 722 us; the launch traced here: 720 us
  blocking collectives  376 us (52%)
  waiting for transfers between devices  189 us (26%)
  starting transfers between devices  77.2 us (11%)
  local copies, waits for them, and re-layouts  41.7 us (6%)
  matrix products  19.5 us (3%)
  between operations  16.4 us (2%)
    unnamed x1, blocking collectives  150 us
    all_gather x1, waiting for transfers between devices, body(): lax.all_gather(conv_filters, 'ctx', axis=2, tiled=True)  122 us
    psum x1, blocking collectives, body(): factor = lax.psum(local_gap, 'ctx') / (2.0 * NOISE_SCALE)  119 us
    all_gather x1, waiting for transfers between devices, body(): lax.all_gather(exit_weight, 'ctx', axis=0, tiled=True)  65.7 us
    unnamed x16, starting transfers between devices  63.3 us
    all_to_all x1, blocking collectives, body(): lax.all_to_all(jnp.stack([entry_weight] * lax.axis_size('ctx')), 'ctx', 0...  54.7 us
    psum x1, blocking collectives, body(): grouped = lax.psum(local_term, 'dp')  52.5 us
    unnamed x23, local copies, waits for them, and re-layouts  25.6 us
  transfers between devices with their start and end apart: 22, of which 3 were waited for; matrix products, arithmetic and copies ran while one was open for 8% of the time, Pallas kernels for 0%

profile of v1, /device:TPU:8, one launch (start us, length us, event | category | flops | bytes accessed | tf_op | source)
XLA Modules:
  0.0 720.0 jit_solution(3280021906698806769)
XLA Ops:
  7.2 0.0 copy-start
  7.2 0.0 all-gather.6.cloned.1.call-start
  7.2 0.7 all-gather.6.cloned.1.call-update
  7.9 0.0 all-gather.4.cloned.1.call-start
  8.0 1.5 copy.10
  9.5 0.0 all-gather.4.cloned.1.call-update
  9.5 0.8 stack.2
  10.4 54.7 %all_to_all.5 = bf16[64,6,1536]{2,1,0:T(8,128)(2,1)S(1)} all-to-all(bf16[64,6,1536]{2,1,0:T(8,128)(2,1)S(1)} %stack.2), channel_id=1, replica_groups=mesh['ctx'=64,'dp'=8] {'ctx'}, dimensions={0} | all-to-all | bytes 2359296 | tf_op jit(solution)/shard_map/all_to_all | solution.py:57
  65.1 1.2 reshape.14
  66.3 3.8 fusion.18
  70.0 0.7 fusion.104
  70.8 3.6 collective-permute-start.3
  74.4 1.9 collective-permute-start.2
  76.3 0.7 fusion.105
  77.0 6.3 collective-permute-start.1
  83.4 1.9 collective-permute-start
  85.3 65.7 %all-gather.6.cloned.1.call-done = bf16[64,6,1536]{2,1,0:T(8,128)(2,1)} async-done(((bf16[1,6,1536]{2,1,0:T(8,128)(2,1)}), bf16[64,6,1536]{2,1,0:T(8,128)(2,1)}) %all-gather.6.cloned.1.call-update) | async-done | bytes 1179664 | tf_op jit(solution)/shard_map/all_gather | solution.py:71
  151.0 3.1 reshape.17
  154.1 122.0 %all-gather.4.cloned.1.call-done = bf16[3,1536,384]{1,0,2:T(4,128)(2,1)} async-done(((bf16[3,1536,6]{1,0,2:T(4,128)(2,1)}), bf16[3,1536,384]{1,0,2:T(4,128)(2,1)}) %all-gather.4.cloned.1.call-update) | async-done | bytes 3538960 | tf_op jit(solution)/shard_map/all_gather | solution.py:67
  276.1 12.7 %fusion.103 = (bf16[1,1536,384]{1,0,2:T(2,128)(2,1)}, bf16[1,1536,384]{1,0,2:T(2,128)(2,1)}, bf16[1,1536,384]{1,0,2:T(2,128)(2,1)}) fusion(bf16[3,1536,384]{1,0,2:T(4,128)(2,1)} %all-gather.4.cloned.1.call-done), kind=kLoop, calls=%fused_computation.97 | loop fusion | bytes 7077888 | tf_op jit(solution)/shard_map/slice | solution.py:28
  288.8 5.6 copy.15
  294.4 0.5 fusion.25
  294.9 6.5 copy.16
  301.4 0.0 collective-permute-done.3
  301.4 2.5 fusion.21
  303.9 5.6 copy.14
  309.6 3.9 convolution_add_fusion
  313.4 1.7 fusion.27
  315.1 0.0 collective-permute-done.1
  315.1 2.2 fusion.23
  317.3 0.0 collective-permute-done
  317.3 4.6 fusion.20
  322.5 119.0 %psum.14 = f32[]{:T(128)} all-reduce(f32[]{:T(128)S(6)} %div.6), channel_id=1, replica_groups=mesh['ctx'=64,'dp'=8] {'ctx'}, use_global_device_ids=true, to_apply=%region_1.0 | all-reduce | flops 1 | bytes 8 | tf_op jit(solution)/shard_map/psum | solution.py:79
  442.1 0.5 convolution_multiply_fusion
  442.6 149.7 %fusion = f32[8,1536]{1,0:T(8,128)S(1)} fusion(f32[384,1536]{1,0:T(8,128)S(1)} %convolution_multiply_fusion), kind=kCustom, calls=%all-reduce-scatter | all-reduce-scatter fusion | flops 786433 | bytes 2410496
  592.3 2.0 collective-permute-start.19
  594.4 21.2 %collective-permute-start.10 = (f32[8,1536]{1,0:T(8,128)S(1)}, f32[8,1536]{1,0:T(8,128)S(1)}, u32[]{:S(2)}, u32[]{:S(2)}) collective-permute-start(f32[8,1536]{1,0:T(8,128)S(1)} %fusion), channel_id=1, source_target_pairs={{0,56},{8,64},{16,72},{24,80},{32,88},{40,96},{48,104},{56,112},{6... | collective-permute-start | bytes 147464
  615.5 5.5 collective-permute-start.11
  621.0 1.9 collective-permute-start.12
  622.9 2.4 collective-permute-start.13
  625.3 0.0 collective-permute-done.19
  625.3 1.3 collective-permute-start.14
  626.6 5.7 collective-permute-start.15
  632.3 1.6 collective-permute-start.16
  634.0 0.0 collective-permute-done.12
  634.0 2.7 collective-permute-start.17
  636.7 0.0 collective-permute-done.13
  636.8 1.4 collective-permute-start.18
  638.1 0.0 collective-permute-done.14
  638.2 2.0 collective-permute-start.4
  640.1 0.0 collective-permute-done.15
  640.1 3.0 collective-permute-start.5
  643.1 2.7 collective-permute-start.6
  645.9 4.1 collective-permute-start.7
  650.0 0.0 collective-permute-done.18
  650.0 1.9 collective-permute-start.8
  651.9 3.9 collective-permute-start.9
  655.8 1.3 dynamic-slice.4
  657.8 0.0 collective-permute-done.5
  657.8 0.0 collective-permute-done.7
  657.8 0.0 collective-permute-done.8
  657.8 1.0 collective-permute-done.9
  658.8 1.9 concatenate.18
  660.7 52.5 %psum.16 = f32[6,1536]{1,0:T(8,128)} all-reduce(f32[6,1536]{1,0:T(8,128)S(1)} %constant_dynamic-slice_fusion), channel_id=1, replica_groups=mesh['ctx'=64,'dp'=8] {'dp'}, use_global_device_ids=true, to_apply=%region_2.0 | all-reduce | flops 9216 | bytes 73728 | tf_op jit(solution)/shard_map/psum | solution.py:83
  (22 shorter events, 0.1 us)
Async XLA Ops:
  7.2 59.1 %copy-start = (bf16[1,192,384]{2,1,0:T(8,128)(2,1)S(1)}, bf16[1,192,384]{2,1,0:T(8,128)(2,1)}, u32[]{:S(2)}) copy-start(bf16[1,192,384]{2,1,0:T(8,128)(2,1)} %param.8) | copy-start | bytes 442372
  7.2 143.8 %all-gather.6.cloned.1.call-start = ((), (), s32[]{:S(2)}) async-start(), calls=%async_computation.2 | async-start | bytes 1597440 | tf_op jit(solution)/shard_map/all_gather | solution.py:71
  7.9 268.2 %all-gather.4.cloned.1.call-start = ((), (), s32[]{:S(2)}) async-start(), calls=%async_computation.1 | async-start | bytes 4792320 | tf_op jit(solution)/shard_map/all_gather | solution.py:67
  65.1 1.2 copy-start.2
  70.0 84.1 %copy-start.4 = (bf16[192,1536]{1,0:T(8,128)(2,1)}, bf16[192,1536]{1,0:T(8,128)(2,1)S(1)}, u32[]{:S(2)}) copy-start(bf16[192,1536]{1,0:T(8,128)(2,1)S(1)} %get-tuple-element.8) | copy-start | bytes 1769476
  70.0 231.4 %copy-start.3 = (bf16[192,1536]{1,0:T(8,128)(2,1)}, bf16[192,1536]{1,0:T(8,128)(2,1)S(1)}, u32[]{:S(2)}) copy-start(bf16[192,1536]{1,0:T(8,128)(2,1)S(1)} %get-tuple-element.7) | copy-start | bytes 1769476
  70.8 230.7 %collective-permute-start.3 = (bf16[32,1536]{1,0:T(8,128)(2,1)}, bf16[32,1536]{1,0:T(8,128)(2,1)}, u32[]{:S(2)}, u32[]{:S(2)}) collective-permute-start(bf16[32,1536]{1,0:T(8,128)(2,1)} %get-tuple-element.10), channel_id=1, source_target_pairs={{8,0},{16,8},{24,16},{32,24},{40,32},{48,40},{56,48},{64,56},{72,6... | collective-permute-start | bytes 294920 | tf_op jit(solution)/shard_map/ppermute | solution.py:20
  74.4 235.1 %collective-permute-start.2 = (bf16[32,1536]{1,0:T(8,128)(2,1)}, bf16[32,1536]{1,0:T(8,128)(2,1)}, u32[]{:S(2)}, u32[]{:S(2)}) collective-permute-start(bf16[32,1536]{1,0:T(8,128)(2,1)} %get-tuple-element.9), channel_id=1, source_target_pairs={{0,8},{8,16},{16,24},{24,32},{32,40},{40,48},{48,56},{56,64},{64,7... | collective-permute-start | bytes 294920 | tf_op jit(solution)/shard_map/ppermute | solution.py:18
  77.0 238.1 %collective-permute-start.1 = (bf16[32,1536]{1,0:T(8,128)(2,1)}, bf16[32,1536]{1,0:T(8,128)(2,1)}, u32[]{:S(2)}, u32[]{:S(2)}) collective-permute-start(bf16[32,1536]{1,0:T(8,128)(2,1)} %get-tuple-element.12), channel_id=1, source_target_pairs={{8,0},{16,8},{24,16},{32,24},{40,32},{48,40},{56,48},{64,56},{72,6... | collective-permute-start | bytes 294920 | tf_op jit(solution)/shard_map/ppermute | solution.py:20
  83.4 233.9 %collective-permute-start = (bf16[32,1536]{1,0:T(8,128)(2,1)}, bf16[32,1536]{1,0:T(8,128)(2,1)S(1)}, u32[]{:S(2)}, u32[]{:S(2)}) collective-permute-start(bf16[32,1536]{1,0:T(8,128)(2,1)} %get-tuple-element.11), channel_id=1, source_target_pairs={{0,8},{8,16},{16,24},{24,32},{32,40},{40,48},{48,56},{56,64},{64,7... | collective-permute-start | bytes 294920 | tf_op jit(solution)/shard_map/ppermute | solution.py:18
  313.4 1.7 copy-start.5
  313.4 1.7 copy-start.6
  315.1 2.2 copy-start.1
  592.3 33.0 %collective-permute-start.19 = (f32[6,1536]{1,0:T(8,128)S(1)}, f32[6,1536]{1,0:T(8,128)S(1)}, u32[]{:S(2)}, u32[]{:S(2)}) collective-permute-start(f32[6,1536]{1,0:T(8,128)S(1)} %slice.58), channel_id=1, source_target_pairs={{0,128},{8,136},{16,144},{24,152},{32,160},{40,168},{48,176},{56,1... | collective-permute-start | bytes 110600
  594.4 32.3 %collective-permute-start.10 = (f32[8,1536]{1,0:T(8,128)S(1)}, f32[8,1536]{1,0:T(8,128)S(1)}, u32[]{:S(2)}, u32[]{:S(2)}) collective-permute-start(f32[8,1536]{1,0:T(8,128)S(1)} %fusion), channel_id=1, source_target_pairs={{0,56},{8,64},{16,72},{24,80},{32,88},{40,96},{48,104},{56,112},{6... | collective-permute-start | bytes 147464
  615.5 16.8 %collective-permute-start.11 = (f32[8,1536]{1,0:T(8,128)S(1)}, f32[8,1536]{1,0:T(8,128)S(1)}, u32[]{:S(2)}, u32[]{:S(2)}) collective-permute-start(f32[8,1536]{1,0:T(8,128)S(1)} %fusion), channel_id=1, source_target_pairs={{0,64},{8,72},{16,80},{24,88},{32,96},{40,104},{48,112},{56,120},{... | collective-permute-start | bytes 147464
  621.0 13.0 %collective-permute-start.12 = (f32[8,1536]{1,0:T(8,128)S(1)}, f32[8,1536]{1,0:T(8,128)S(1)}, u32[]{:S(2)}, u32[]{:S(2)}) collective-permute-start(f32[8,1536]{1,0:T(8,128)S(1)} %fusion), channel_id=1, source_target_pairs={{0,72},{8,80},{16,88},{24,96},{32,104},{40,112},{48,120},{56,128},... | collective-permute-start | bytes 147464
  622.9 13.8 %collective-permute-start.13 = (f32[8,1536]{1,0:T(8,128)S(1)}, f32[8,1536]{1,0:T(8,128)S(1)}, u32[]{:S(2)}, u32[]{:S(2)}) collective-permute-start(f32[8,1536]{1,0:T(8,128)S(1)} %fusion), channel_id=1, source_target_pairs={{0,80},{8,88},{16,96},{24,104},{32,112},{40,120},{48,128},{56,136}... | collective-permute-start | bytes 147464
  625.3 12.8 %collective-permute-start.14 = (f32[8,1536]{1,0:T(8,128)S(1)}, f32[8,1536]{1,0:T(8,128)S(1)}, u32[]{:S(2)}, u32[]{:S(2)}) collective-permute-start(f32[8,1536]{1,0:T(8,128)S(1)} %fusion), channel_id=1, source_target_pairs={{0,88},{8,96},{16,104},{24,112},{32,120},{40,128},{48,136},{56,144... | collective-permute-start | bytes 147464
  626.6 13.5 %collective-permute-start.15 = (f32[8,1536]{1,0:T(8,128)S(1)}, f32[8,1536]{1,0:T(8,128)S(1)}, u32[]{:S(2)}, u32[]{:S(2)}) collective-permute-start(f32[8,1536]{1,0:T(8,128)S(1)} %fusion), channel_id=1, source_target_pairs={{0,96},{8,104},{16,112},{24,120},{32,128},{40,136},{48,144},{56,15... | collective-permute-start | bytes 147464
  632.3 10.8 %collective-permute-start.16 = (f32[8,1536]{1,0:T(8,128)S(1)}, f32[8,1536]{1,0:T(8,128)S(1)}, u32[]{:S(2)}, u32[]{:S(2)}) collective-permute-start(f32[8,1536]{1,0:T(8,128)S(1)} %fusion), channel_id=1, source_target_pairs={{0,104},{8,112},{16,120},{24,128},{32,136},{40,144},{48,152},{56,1... | collective-permute-start | bytes 147464
  634.0 11.9 %collective-permute-start.17 = (f32[8,1536]{1,0:T(8,128)S(1)}, f32[8,1536]{1,0:T(8,128)S(1)}, u32[]{:S(2)}, u32[]{:S(2)}) collective-permute-start(f32[8,1536]{1,0:T(8,128)S(1)} %fusion), channel_id=1, source_target_pairs={{0,112},{8,120},{16,128},{24,136},{32,144},{40,152},{48,160},{56,1... | collective-permute-start | bytes 147464
  636.8 13.2 %collective-permute-start.18 = (f32[8,1536]{1,0:T(8,128)S(1)}, f32[8,1536]{1,0:T(8,128)S(1)}, u32[]{:S(2)}, u32[]{:S(2)}) collective-permute-start(f32[8,1536]{1,0:T(8,128)S(1)} %fusion), channel_id=1, source_target_pairs={{0,120},{8,128},{16,136},{24,144},{32,152},{40,160},{48,168},{56,1... | collective-permute-start | bytes 147464
  638.2 13.8 %collective-permute-start.4 = (f32[8,1536]{1,0:T(8,128)S(1)}, f32[8,1536]{1,0:T(8,128)S(1)}, u32[]{:S(2)}, u32[]{:S(2)}) collective-permute-start(f32[8,1536]{1,0:T(8,128)S(1)} %fusion), channel_id=1, source_target_pairs={{0,8},{8,16},{16,24},{24,32},{32,40},{40,48},{48,56},{56,64},{64,7... | collective-permute-start | bytes 147464
  640.1 17.6 %collective-permute-start.5 = (f32[8,1536]{1,0:T(8,128)S(1)}, f32[8,1536]{1,0:T(8,128)S(1)}, u32[]{:S(2)}, u32[]{:S(2)}) collective-permute-start(f32[8,1536]{1,0:T(8,128)S(1)} %fusion), channel_id=1, source_target_pairs={{0,16},{8,24},{16,32},{24,40},{32,48},{40,56},{48,64},{56,72},{64,... | collective-permute-start | bytes 147464
  643.1 14.7 %collective-permute-start.6 = (f32[8,1536]{1,0:T(8,128)S(1)}, f32[8,1536]{1,0:T(8,128)S(1)}, u32[]{:S(2)}, u32[]{:S(2)}) collective-permute-start(f32[8,1536]{1,0:T(8,128)S(1)} %fusion), channel_id=1, source_target_pairs={{0,24},{8,32},{16,40},{24,48},{32,56},{40,64},{48,72},{56,80},{64,... | collective-permute-start | bytes 147464
  645.9 11.9 %collective-permute-start.7 = (f32[8,1536]{1,0:T(8,128)S(1)}, f32[8,1536]{1,0:T(8,128)S(1)}, u32[]{:S(2)}, u32[]{:S(2)}) collective-permute-start(f32[8,1536]{1,0:T(8,128)S(1)} %fusion), channel_id=1, source_target_pairs={{0,32},{8,40},{16,48},{24,56},{32,64},{40,72},{48,80},{56,88},{64,... | collective-permute-start | bytes 147464
  650.0 7.8 %collective-permute-start.8 = (f32[8,1536]{1,0:T(8,128)S(1)}, f32[8,1536]{1,0:T(8,128)S(1)}, u32[]{:S(2)}, u32[]{:S(2)}) collective-permute-start(f32[8,1536]{1,0:T(8,128)S(1)} %fusion), channel_id=1, source_target_pairs={{0,40},{8,48},{16,56},{24,64},{32,72},{40,80},{48,88},{56,96},{64,... | collective-permute-start | bytes 147464
  651.9 6.9 collective-permute-start.9
Sparse Core Ops, SparseCore 0:
  10.2 140.8 all-gather.5
  153.2 122.9 all-gather.3
